TPU v7x, 128 devices: a whole 4x4x4 slice. The times are simulated.
128 devices in a mesh: space: 32 (over x, z, core), feat: 4 (over y).
Axes of the slice: x: 4, y: 4, z: 4, core: 2. Of those that a mesh axis runs over, the one named last changes fastest.
Arguments:
- inputs: bfloat16 [2, 96, 180, 1024], P(None, 'space', None, 'feat'), may hold values from -15 to 15
- cotangent: bfloat16 [2, 96, 180, 1024], P(None, 'space', None, 'feat'), may hold values from -6 to 6
- spec_w1: float32 [2, 8, 128, 128], P(None, 'feat'), may hold values from -0.375 to 0.375
- spec_b1: float32 [2, 1024], P(None, 'feat'), may hold values from -0.3 to 0.3
- spec_w2: float32 [2, 8, 128, 128], P(None, 'feat'), may hold values from -0.375 to 0.375
- spec_b2: float32 [2, 1024], P(None, 'feat'), may hold values from -0.3 to 0.3
- up_weight: bfloat16 [1024, 4096], P(None, 'feat'), may hold values from -0.1875 to 0.1875
- down_weight: bfloat16 [4096, 1024], P('feat'), may hold values from -0.09375 to 0.09375
Outputs:
- output: bfloat16 [2, 96, 180, 1024], P(None, 'space', None, 'feat')
- grad_input: bfloat16 [2, 96, 180, 1024], P(None, 'space', None, 'feat')
All inputs are finite; a program needn't handle non-finite values.
Results may differ from a plain program's by a relative error of at most 0.0102.
Values may be sent and summed in bfloat16 or wider, within the bound.
No kernel may reach another device: no remote copies, remote signals or barrier semaphores. Data moves between devices by JAX's collectives and lax.ppermute only.
A program may use at most 128 MiB of HBM per device.

v0:
```python
import math
import jax
import jax.numpy as jnp
from jax import lax
from jax.sharding import PartitionSpec as P

EPSILON = 1e-05
SHRINK_LEVEL = 0.1
HIGHEST = lax.Precision.HIGHEST


def longitude_tables(width_lon):
    mode_count = width_lon // 2 + 1
    cell_index = jnp.arange(width_lon, dtype=jnp.int32)[:, None]
    wave_number = jnp.arange(mode_count, dtype=jnp.int32)[None, :]
    phase_angle = (
        2.0 * math.pi / width_lon * (cell_index * wave_number % width_lon).astype(jnp.float32)
    )
    scaling = 1.0 / math.sqrt(width_lon)
    cos_fwd = jnp.cos(phase_angle) * scaling
    sin_fwd = -jnp.sin(phase_angle) * scaling
    doubled = jnp.where((wave_number == 0) | (wave_number * 2 == width_lon), 1.0, 2.0).astype(
        jnp.float32
    )
    return (cos_fwd, sin_fwd, cos_fwd * doubled, sin_fwd * doubled)


def padded_tables(width_lon, multiple):
    tables = longitude_tables(width_lon)
    modes = tables[0].shape[1]
    extra = -modes % multiple
    return tuple((jnp.pad(table, ((0, 0), (0, extra))) for table in tables))


def lat_apply(table, field):
    return jnp.einsum("gh,bhkc->bgkc", table, field, precision=HIGHEST)


def complex_latitude(table_cos, table_sin, real_part, imag_part, inverse):
    if inverse:
        return (
            lat_apply(table_cos, real_part) + lat_apply(table_sin, imag_part),
            lat_apply(table_cos, imag_part) - lat_apply(table_sin, real_part),
        )
    return (
        lat_apply(table_cos, real_part) - lat_apply(table_sin, imag_part),
        lat_apply(table_cos, imag_part) + lat_apply(table_sin, real_part),
    )


def lon_forward(field, table):
    return jnp.einsum("brwc,wk->brkc", field, table, precision=HIGHEST)


def lon_back(spec, table):
    return jnp.einsum("brkc,wk->brwc", spec, table, precision=HIGHEST)


def to_blocks(field, block_size):
    return field.reshape(field.shape[:-1] + (field.shape[-1] // block_size, block_size))


def block_mult(field, weights):
    return jnp.einsum("...nc,nce->...ne", field, weights, precision=HIGHEST)


def block_mult_back(field, weights):
    return jnp.einsum("...ne,nce->...nc", field, weights, precision=HIGHEST)


def block_product(real_part, imag_part, weights):
    return (
        block_mult(real_part, weights[0]) - block_mult(imag_part, weights[1]),
        block_mult(real_part, weights[1]) + block_mult(imag_part, weights[0]),
    )


def block_adjoint(real_part, imag_part, weights):
    return (
        block_mult_back(real_part, weights[0]) + block_mult_back(imag_part, weights[1]),
        block_mult_back(imag_part, weights[0]) - block_mult_back(real_part, weights[1]),
    )


def latitude_tables(length):
    index_row = jnp.arange(length, dtype=jnp.int32)
    phase_angle = (
        2.0
        * math.pi
        / length
        * (index_row[:, None] * index_row[None, :] % length).astype(jnp.float32)
    )
    scaling = 1.0 / math.sqrt(length)
    return (jnp.cos(phase_angle) * scaling, -jnp.sin(phase_angle) * scaling)


def to_columns(real_part, imag_part):
    stacked = jnp.stack([real_part, imag_part])
    moved = lax.all_to_all(stacked, "space", 3, 2, tiled=True)
    return (moved[0], moved[1])


def to_rows(real_part, imag_part):
    stacked = jnp.stack([real_part, imag_part])
    moved = lax.all_to_all(stacked, "space", 2, 3, tiled=True)
    return (moved[0], moved[1])


def enter_spectrum(real_part, imag_part):
    length = real_part.shape[1] * lax.axis_size("space")
    table_cos, table_sin = latitude_tables(length)
    real_part, imag_part = to_columns(real_part, imag_part)
    return complex_latitude(table_cos, table_sin, real_part, imag_part, False)


def leave_spectrum(real_part, imag_part):
    table_cos, table_sin = latitude_tables(real_part.shape[1])
    real_part, imag_part = complex_latitude(table_cos, table_sin, real_part, imag_part, True)
    return to_rows(real_part, imag_part)


def token_sums(first_term, second_term):
    pair = jnp.stack([first_term, second_term])
    count = lax.axis_size("feat")
    bit = 1
    while bit < count:
        pair = pair + lax.ppermute(pair, "feat", [(i, i ^ bit) for i in range(count)])
        bit *= 2
    return (pair[0], pair[1])


def ring_send(block):
    count = lax.axis_size("feat")
    return [block] + [
        lax.ppermute(block, "feat", [(i, (i + shift) % count) for i in range(count)])
        for shift in range(1, count)
    ]


def ring_assemble(parts):
    count = len(parts)
    position = lax.axis_index("feat")
    block = parts[0]
    width = block.shape[-1]
    whole = jnp.zeros(block.shape[:-1] + (width * count,), block.dtype)
    for shift, moved in enumerate(parts):
        source = (position + count - shift) % count
        whole = lax.dynamic_update_slice_in_dim(whole, moved, source * width, axis=block.ndim - 1)
    return whole


def channel_share(term):
    return lax.psum_scatter(
        term.astype(jnp.bfloat16), "feat", scatter_dimension=3, tiled=True
    ).astype(jnp.float32)


def gelu_value(field):
    return 0.5 * field * (1.0 + lax.erf(field * (1.0 / math.sqrt(2.0))))


def gelu_slope(field):
    return 0.5 * (1.0 + lax.erf(field * (1.0 / math.sqrt(2.0)))) + field * jnp.exp(
        -0.5 * field * field
    ) * (1.0 / math.sqrt(2.0 * math.pi))


def spectral_forward(field, spec_w1, spec_b1, spec_w2, spec_b2, cos_fwd, sin_fwd):
    block_size = spec_w1.shape[2]
    spec_real, spec_imag = enter_spectrum(lon_forward(field, cos_fwd), lon_forward(field, sin_fwd))
    spec_shape = spec_real.shape
    bias_one = to_blocks(spec_b1, block_size)
    bias_two = to_blocks(spec_b2, block_size)
    first_real, first_imag = block_product(
        to_blocks(spec_real, block_size), to_blocks(spec_imag, block_size), spec_w1
    )
    first_real = jax.nn.relu(first_real + bias_one[0])
    first_imag = jax.nn.relu(first_imag + bias_one[1])
    second_real, second_imag = block_product(first_real, first_imag, spec_w2)
    second_real = second_real + bias_two[0]
    second_imag = second_imag + bias_two[1]
    shrunk_real = (second_real - jnp.clip(second_real, -SHRINK_LEVEL, SHRINK_LEVEL)).reshape(
        spec_shape
    )
    shrunk_imag = (second_imag - jnp.clip(second_imag, -SHRINK_LEVEL, SHRINK_LEVEL)).reshape(
        spec_shape
    )
    back = complex_latitude_inverse(shrunk_real, shrunk_imag)
    return (back, (first_real, first_imag, second_real, second_imag))


def complex_latitude_inverse(real_part, imag_part):
    table_cos, table_sin = latitude_tables(real_part.shape[1])
    return complex_latitude(table_cos, table_sin, real_part, imag_part, True)


def spectral_leave(back, cos_inv, sin_inv):
    back_real, back_imag = to_rows(*back)
    return lon_back(back_real, cos_inv) + lon_back(back_imag, sin_inv)


def spectral_backward(grad_field, saved, spec_w1, spec_w2, cos_fwd, sin_fwd, cos_inv, sin_inv):
    block_size = spec_w1.shape[2]
    first_real, first_imag, second_real, second_imag = saved
    grad_real, grad_imag = enter_spectrum(
        lon_forward(grad_field, cos_inv), lon_forward(grad_field, sin_inv)
    )
    spec_shape = grad_real.shape
    grad_real = jnp.where(
        jnp.abs(second_real) > SHRINK_LEVEL, to_blocks(grad_real, block_size), 0.0
    )
    grad_imag = jnp.where(
        jnp.abs(second_imag) > SHRINK_LEVEL, to_blocks(grad_imag, block_size), 0.0
    )
    first_grad_real, first_grad_imag = block_adjoint(grad_real, grad_imag, spec_w2)
    first_grad_real = jnp.where(first_real > 0.0, first_grad_real, 0.0)
    first_grad_imag = jnp.where(first_imag > 0.0, first_grad_imag, 0.0)
    spec_grad_real, spec_grad_imag = block_adjoint(first_grad_real, first_grad_imag, spec_w1)
    rows_real, rows_imag = leave_spectrum(
        spec_grad_real.reshape(spec_shape), spec_grad_imag.reshape(spec_shape)
    )
    return lon_back(rows_real, cos_fwd) + lon_back(rows_imag, sin_fwd)


def per_device(inputs, cotangent, spec_w1, spec_b1, spec_w2, spec_b2, up_weight, down_weight):
    full_width = up_weight.shape[0]
    block_size = spec_w1.shape[2]
    cos_fwd, sin_fwd, cos_inv, sin_inv = padded_tables(inputs.shape[2], lax.axis_size("space"))
    values = inputs.astype(jnp.float32)
    cotangent_parts = ring_send(cotangent)
    first_sum, second_sum = token_sums(jnp.sum(values, axis=-1), jnp.sum(values * values, axis=-1))
    mean_one = first_sum[..., None] / full_width
    rstd_one = lax.rsqrt(second_sum[..., None] / full_width - mean_one * mean_one + EPSILON)
    normed = (values - mean_one) * rstd_one
    block_count = spec_w1.shape[1]
    shrunk_parts, saved_parts = ([], [])
    for block in range(block_count):
        channels = slice(block * block_size, (block + 1) * block_size)
        shrunk, saved = spectral_forward(
            normed[..., channels],
            spec_w1[:, block : block + 1],
            spec_b1[:, channels],
            spec_w2[:, block : block + 1],
            spec_b2[:, channels],
            cos_fwd,
            sin_fwd,
        )
        shrunk_parts.append(shrunk)
        saved_parts.append(saved)
    shrunk_parts[-1], cotangent_parts = lax.optimization_barrier(
        (shrunk_parts[-1], cotangent_parts)
    )
    whole_cotangent = ring_assemble(cotangent_parts)
    filtered = jnp.concatenate(
        [spectral_leave(shrunk, cos_inv, sin_inv) for shrunk in shrunk_parts], axis=-1
    )
    residual = (filtered + normed + values).astype(jnp.bfloat16)
    residual_vals = residual.astype(jnp.float32)
    whole_residual = lax.all_gather(residual, "feat", axis=3, tiled=True)
    whole_vals = whole_residual.astype(jnp.float32)
    mean_two = jnp.sum(whole_vals, axis=-1, keepdims=True) / full_width
    square_two = jnp.sum(whole_vals * whole_vals, axis=-1, keepdims=True) / full_width
    rstd_two = lax.rsqrt(square_two - mean_two * mean_two + EPSILON)
    vhat = (whole_vals - mean_two) * rstd_two
    hidden = jnp.einsum(
        "brwd,dh->brwh", vhat.astype(jnp.bfloat16), up_weight, preferred_element_type=jnp.float32
    )
    activated = gelu_value(hidden).astype(jnp.bfloat16)
    mixed_term = jnp.einsum(
        "brwh,hd->brwd", activated, down_weight, preferred_element_type=jnp.float32
    )
    output = (residual_vals + channel_share(mixed_term)).astype(jnp.bfloat16)
    grad_act = jnp.einsum(
        "brwd,hd->brwh", whole_cotangent, down_weight, preferred_element_type=jnp.float32
    )
    grad_hidden = (grad_act * gelu_slope(hidden)).astype(jnp.bfloat16)
    grad_term = jnp.einsum(
        "brwh,dh->brwd", grad_hidden, up_weight, preferred_element_type=jnp.float32
    )
    total_one, total_two = token_sums(
        jnp.sum(grad_term, axis=-1), jnp.sum(grad_term * vhat, axis=-1)
    )
    grad_vhat = channel_share(grad_term)
    own_hat = (residual_vals - mean_two) * rstd_two
    grad_residual = cotangent.astype(jnp.float32) + rstd_two * (
        grad_vhat
        - total_one[..., None] / full_width
        - own_hat * (total_two[..., None] / full_width)
    )
    grad_filter = jnp.concatenate(
        [
            spectral_backward(
                grad_residual[..., block * block_size : (block + 1) * block_size],
                saved_parts[block],
                spec_w1[:, block : block + 1],
                spec_w2[:, block : block + 1],
                cos_fwd,
                sin_fwd,
                cos_inv,
                sin_inv,
            )
            for block in range(block_count)
        ],
        axis=-1,
    )
    grad_normed = grad_residual + grad_filter
    norm_one, norm_two = token_sums(
        jnp.sum(grad_normed, axis=-1), jnp.sum(grad_normed * normed, axis=-1)
    )
    grad_input = grad_residual + rstd_one * (
        grad_normed - norm_one[..., None] / full_width - normed * (norm_two[..., None] / full_width)
    )
    return (output, grad_input.astype(jnp.bfloat16))


def solution(mesh):
    return jax.shard_map(
        per_device,
        mesh=mesh,
        in_specs=(
            P(None, "space", None, "feat"),
            P(None, "space", None, "feat"),
            P(None, "feat", None, None),
            P(None, "feat"),
            P(None, "feat", None, None),
            P(None, "feat"),
            P(None, "feat"),
            P("feat", None),
        ),
        out_specs=(P(None, "space", None, "feat"), P(None, "space", None, "feat")),
        check_vma=False,
    )
```

profile of v0, /device:TPU:0, one launch (start us, length us, event | category | flops | bytes accessed | tf_op | source)
XLA Modules:
  0.0 356.5 jit_solution(820768273294857177)
XLA Ops:
  7.2 3.2 collective-permute-start.4
  17.2 17.8 %collective-permute-done = f32[2,2,3,180]{3,2,1,0:T(4,128)S(1)} collective-permute-done((f32[2,2,3,180]{3,2,1,0:T(4,128)S(1)}, f32[2,2,3,180]{3,2,1,0:T(4,128)S(1)}, u32[]{:S(2)}, u32[]{:S(2)}) %collective-permute-start) | collective-permute-done | bytes 8672 | tf_op jit(solution)/shard_map/ppermute | solution.py:127
  35.0 3.1 collective-permute-start.1
  44.0 8.3 %all-to-all-start = ((f32[2,2,3,96,128]{4,1,2,0,3:T(2,128)}), f32[2,2,3,96,128]{4,1,2,0,3:T(2,128)}, u32[]{:S(2)}, u32[]{:S(2)}) async-start(f32[2,2,3,96,128]{4,1,2,0,3:T(2,128)} %copy.147), calls=%async_computation | async-start | bytes 1179648 | tf_op jit(solution)/shard_map/all_to_all | solution.py:99
  55.2 8.9 %all-to-all-done = f32[2,2,3,96,128]{4,1,2,0,3:T(2,128)} async-done(((f32[2,2,3,96,128]{4,1,2,0,3:T(2,128)}), f32[2,2,3,96,128]{4,1,2,0,3:T(2,128)}, u32[]{:S(2)}, u32[]{:S(2)}) %all-to-all-start) | async-done | bytes 589856 | tf_op jit(solution)/shard_map/all_to_all | solution.py:99
  64.1 4.6 %all-to-all-start.2 = ((f32[2,2,3,96,128]{4,1,2,0,3:T(2,128)}), f32[2,2,3,96,128]{4,1,2,0,3:T(2,128)S(1)}, u32[]{:S(2)}, u32[]{:S(2)}) async-start(f32[2,2,3,96,128]{4,1,2,0,3:T(2,128)} %copy.161), calls=%async_computation.2 | async-start | bytes 1179648 | tf_op jit(solution)/shard_map/all_to_all | solution.py:99
  92.2 4.6 %all-to-all-start.1 = ((f32[2,2,96,3,128]{4,1,3,0,2:T(2,128)}), f32[2,2,96,3,128]{4,1,3,0,2:T(2,128)}, u32[]{:S(2)}, u32[]{:S(2)}) async-start(f32[2,2,96,3,128]{4,1,3,0,2:T(2,128)} %copy.155), calls=%async_computation.1 | async-start | bytes 1179648 | tf_op jit(solution)/shard_map/all_to_all | solution.py:105
  103.0 5.5 %all-to-all-done.1 = f32[2,2,96,3,128]{4,1,3,0,2:T(2,128)} async-done(((f32[2,2,96,3,128]{4,1,3,0,2:T(2,128)}), f32[2,2,96,3,128]{4,1,3,0,2:T(2,128)}, u32[]{:S(2)}, u32[]{:S(2)}) %all-to-all-start.1) | async-done | bytes 589856 | tf_op jit(solution)/shard_map/all_to_all | solution.py:105
  108.5 4.1 %all-to-all-start.3 = ((f32[2,2,96,3,128]{4,1,3,0,2:T(2,128)}), f32[2,2,96,3,128]{4,1,3,0,2:T(2,128)S(1)}, u32[]{:S(2)}, u32[]{:S(2)}) async-start(f32[2,2,96,3,128]{4,1,3,0,2:T(2,128)} %copy.169), calls=%async_computation.3 | async-start | bytes 1179648 | tf_op jit(solution)/shard_map/all_to_all | solution.py:105
  115.6 8.9 %all-to-all-done.3 = f32[2,2,96,3,128]{4,1,3,0,2:T(2,128)S(1)} async-done(((f32[2,2,96,3,128]{4,1,3,0,2:T(2,128)}), f32[2,2,96,3,128]{4,1,3,0,2:T(2,128)S(1)}, u32[]{:S(2)}, u32[]{:S(2)}) %all-to-all-start.3) | async-done | bytes 589856 | tf_op jit(solution)/shard_map/all_to_all | solution.py:105
  137.9 26.5 %all-gather.2.cloned.1.call-done = bf16[2,3,180,1024]{3,2,1,0:T(8,128)(2,1)} async-done(((bf16[2,3,180,256]{3,2,1,0:T(8,128)(2,1)}), bf16[2,3,180,1024]{3,2,1,0:T(8,128)(2,1)}) %all-gather.2.cloned.1.call-update) | async-done | bytes 2211856 | tf_op jit(solution)/shard_map/all_gather | solution.py:259
  167.1 5.0 %fusion.14 = f32[2,3,180,1024]{3,2,1,0:T(8,128)} fusion(bf16[2,3,180,1024]{3,2,1,0:T(8,128)(2,1)S(1)} %copy-done.32, f32[2,3,180]{2,1,0:T(4,128)S(1)} %get-tuple-element.54, f32[2,3,180]{2,1,0:T(4,128)S(1)} %get-tuple-element.53, bf16[1024,1024]{1,0:T(8,128)(2,1)S(1)} %copy-done), kind=kOutput, calls=%fused_computation.19 | convolution fusion | flops 2269347840 | bytes 8741312 | tf_op jit(solution)/shard_map/brwd,dh->brwh/dot_general | solution.py:265
  172.1 11.0 %fusion.552 = (f32[2,3,180]{2,1,0:T(4,128)S(1)}, f32[2,3,180]{2,1,0:T(4,128)S(1)}, bf16[2,3,180,1024]{3,2,1,0:T(8,128)(2,1)}) fusion(f32[2,3,180]{2,1,0:T(4,128)S(1)} %get-tuple-element.54, f32[2,3,180]{2,1,0:T(4,128)S(1)} %get-tuple-element.53, bf16[2,3,180,1024]{3,2,1,0:T(8,128)(2,1)} %all-gather.2.cloned.1.call-done, ...), kind=kOutput, calls=%fused_computation.644 | convolution fusion | flops 4548646912 | bytes 15270784 | tf_op jit(solution)/shard_map/brwh,dh->brwd/dot_general | solution.py:277
  184.7 6.2 %fusion.27 = bf16[2,3,180,1024]{3,2,1,0:T(8,128)(2,1)} fusion(bf16[1024,1024]{1,0:T(8,128)(2,1)S(1)} %copy-done.45, f32[2,3,180,1024]{3,2,1,0:T(8,128)} %fusion.14), kind=kOutput, calls=%fused_computation.35 | convolution fusion | flops 2271559680 | bytes 8732672 | tf_op jit(solution)/shard_map/brwh,hd->brwd/dot_general | solution.py:269
  200.4 15.2 %reduce-scatter.5.cloned.1.call-done = bf16[2,3,180,256]{3,2,1,0:T(8,128)(2,1)} async-done(((bf16[2,3,180,1024]{3,2,1,0:T(8,128)(2,1)}), bf16[2,3,180,256]{3,2,1,0:T(8,128)(2,1)}) %reduce-scatter.5.cloned.1.call-update) | async-done | bytes 552976 | tf_op jit(solution)/shard_map/reduce_scatter | solution.py:153
  215.6 33.3 %reduce-scatter.3.cloned.1.call-done = bf16[2,3,180,256]{3,2,1,0:T(8,128)(2,1)} async-done(((bf16[2,3,180,1024]{3,2,1,0:T(8,128)(2,1)}), bf16[2,3,180,256]{3,2,1,0:T(8,128)(2,1)}) %reduce-scatter.3.cloned.1.call-update) | async-done | bytes 552976 | tf_op jit(solution)/shard_map/reduce_scatter | solution.py:153
  253.7 7.6 %all-to-all-start.6 = ((f32[2,2,3,96,128]{4,1,2,0,3:T(2,128)}), f32[2,2,3,96,128]{4,1,2,0,3:T(2,128)S(1)}, u32[]{:S(2)}, u32[]{:S(2)}) async-start(f32[2,2,3,96,128]{4,1,2,0,3:T(2,128)} %copy.194), calls=%async_computation.8 | async-start | bytes 1179648 | tf_op jit(solution)/shard_map/all_to_all | solution.py:99
  263.7 9.5 %all-to-all-done.6 = f32[2,2,3,96,128]{4,1,2,0,3:T(2,128)S(1)} async-done(((f32[2,2,3,96,128]{4,1,2,0,3:T(2,128)}), f32[2,2,3,96,128]{4,1,2,0,3:T(2,128)S(1)}, u32[]{:S(2)}, u32[]{:S(2)}) %all-to-all-start.6) | async-done | bytes 589856 | tf_op jit(solution)/shard_map/all_to_all | solution.py:99
  273.2 4.1 %all-to-all-start.4 = ((f32[2,2,3,96,128]{4,1,2,0,3:T(2,128)}), f32[2,2,3,96,128]{4,1,2,0,3:T(2,128)S(1)}, u32[]{:S(2)}, u32[]{:S(2)}) async-start(f32[2,2,3,96,128]{4,1,2,0,3:T(2,128)} %copy.180), calls=%async_computation.6 | async-start | bytes 1179648 | tf_op jit(solution)/shard_map/all_to_all | solution.py:99
  278.6 10.6 %all-to-all-done.4 = f32[2,2,3,96,128]{4,1,2,0,3:T(2,128)S(1)} async-done(((f32[2,2,3,96,128]{4,1,2,0,3:T(2,128)}), f32[2,2,3,96,128]{4,1,2,0,3:T(2,128)S(1)}, u32[]{:S(2)}, u32[]{:S(2)}) %all-to-all-start.4) | async-done | bytes 589856 | tf_op jit(solution)/shard_map/all_to_all | solution.py:99
  299.7 4.9 %all-to-all-start.5 = ((f32[2,2,96,3,128]{4,1,3,0,2:T(2,128)}), f32[2,2,96,3,128]{4,1,3,0,2:T(2,128)}, u32[]{:S(2)}, u32[]{:S(2)}) async-start(f32[2,2,96,3,128]{4,1,3,0,2:T(2,128)} %copy.188), calls=%async_computation.7 | async-start | bytes 1179648 | tf_op jit(solution)/shard_map/all_to_all | solution.py:105
  316.4 6.9 %all-to-all-start.7 = ((f32[2,2,96,3,128]{4,1,3,0,2:T(2,128)}), f32[2,2,96,3,128]{4,1,3,0,2:T(2,128)S(1)}, u32[]{:S(2)}, u32[]{:S(2)}) async-start(f32[2,2,96,3,128]{4,1,3,0,2:T(2,128)} %copy.202), calls=%async_computation.9 | async-start | bytes 1179648 | tf_op jit(solution)/shard_map/all_to_all | solution.py:105
  325.6 9.5 %all-to-all-done.7 = f32[2,2,96,3,128]{4,1,3,0,2:T(2,128)S(1)} async-done(((f32[2,2,96,3,128]{4,1,3,0,2:T(2,128)}), f32[2,2,96,3,128]{4,1,3,0,2:T(2,128)S(1)}, u32[]{:S(2)}, u32[]{:S(2)}) %all-to-all-start.7) | async-done | bytes 589856 | tf_op jit(solution)/shard_map/all_to_all | solution.py:105
  338.8 3.5 collective-permute-done.7
  (276 shorter events, 117.6 us)
Async XLA Ops:
  7.2 159.9 %copy-start = (bf16[1024,1024]{1,0:T(8,128)(2,1)S(1)}, bf16[1024,1024]{1,0:T(8,128)(2,1)}, u32[]{:S(2)}) copy-start(bf16[1024,1024]{1,0:T(8,128)(2,1)} %param.14) | copy-start | bytes 6291460
  7.2 94.4 %collective-permute-start.4 = (bf16[2,3,180,256]{3,0,2,1:T(2,128)(2,1)}, bf16[2,3,180,256]{3,0,2,1:T(2,128)(2,1)}, u32[]{:S(2)}, u32[]{:S(2)}) collective-permute-start(bf16[2,3,180,256]{3,0,2,1:T(2,128)(2,1)} %param.9), channel_id=1, source_target_pairs={{0,3},{1,0},{2,1},{3,2},{4,7},{5,4},{6,5},{7,6},{8,11},{9,8},{10,9... | collective-permute-start | bytes 1658888 | tf_op jit(solution)/shard_map/ppermute | solution.py:135
  10.3 91.3 %collective-permute-start.3 = (bf16[2,3,180,256]{3,0,2,1:T(2,128)(2,1)}, bf16[2,3,180,256]{3,0,2,1:T(2,128)(2,1)}, u32[]{:S(2)}, u32[]{:S(2)}) collective-permute-start(bf16[2,3,180,256]{3,0,2,1:T(2,128)(2,1)} %param.9), channel_id=1, source_target_pairs={{0,2},{1,3},{2,0},{3,1},{4,6},{5,7},{6,4},{7,5},{8,10},{9,11},{10,... | collective-permute-start | bytes 1658888 | tf_op jit(solution)/shard_map/ppermute | solution.py:135
  11.0 90.7 %collective-permute-start.2 = (bf16[2,3,180,256]{3,0,2,1:T(2,128)(2,1)}, bf16[2,3,180,256]{3,0,2,1:T(2,128)(2,1)}, u32[]{:S(2)}, u32[]{:S(2)}) collective-permute-start(bf16[2,3,180,256]{3,0,2,1:T(2,128)(2,1)} %param.9), channel_id=1, source_target_pairs={{0,1},{1,2},{2,3},{3,0},{4,5},{5,6},{6,7},{7,4},{8,9},{9,10},{10,1... | collective-permute-start | bytes 1658888 | tf_op jit(solution)/shard_map/ppermute | solution.py:135
  13.5 21.4 %collective-permute-start = (f32[2,2,3,180]{3,2,1,0:T(4,128)S(1)}, f32[2,2,3,180]{3,2,1,0:T(4,128)S(1)}, u32[]{:S(2)}, u32[]{:S(2)}) collective-permute-start(f32[2,2,3,180]{3,2,1,0:T(4,128)S(1)} %pad_maximum_fusion.8), channel_id=1, source_target_pairs={{0,1},{1,0},{2,3},{3,2},{4,5},{5,4},{6,7},{7,6},{8,9},{9,8},{10,11... | collective-permute-start | bytes 25928 | tf_op jit(solution)/shard_map/ppermute | solution.py:127
  35.0 5.3 %collective-permute-start.1 = (f32[2,2,3,180]{3,2,1,0:T(4,128)S(1)}, f32[2,2,3,180]{3,2,1,0:T(4,128)S(1)}, u32[]{:S(2)}, u32[]{:S(2)}) collective-permute-start(f32[2,2,3,180]{3,2,1,0:T(4,128)S(1)} %fusion.551), channel_id=1, source_target_pairs={{0,2},{1,3},{2,0},{3,1},{4,6},{5,7},{6,4},{7,5},{8,10},{9,11},{10,... | collective-permute-start | bytes 25928 | tf_op jit(solution)/shard_map/ppermute | solution.py:127
  44.0 20.1 %all-to-all-start = ((f32[2,2,3,96,128]{4,1,2,0,3:T(2,128)}), f32[2,2,3,96,128]{4,1,2,0,3:T(2,128)}, u32[]{:S(2)}, u32[]{:S(2)}) async-start(f32[2,2,3,96,128]{4,1,2,0,3:T(2,128)} %copy.147), calls=%async_computation | async-start | bytes 1179648 | tf_op jit(solution)/shard_map/all_to_all | solution.py:99
  64.1 16.0 %all-to-all-start.2 = ((f32[2,2,3,96,128]{4,1,2,0,3:T(2,128)}), f32[2,2,3,96,128]{4,1,2,0,3:T(2,128)S(1)}, u32[]{:S(2)}, u32[]{:S(2)}) async-start(f32[2,2,3,96,128]{4,1,2,0,3:T(2,128)} %copy.161), calls=%async_computation.2 | async-start | bytes 1179648 | tf_op jit(solution)/shard_map/all_to_all | solution.py:99
  92.2 16.4 %all-to-all-start.1 = ((f32[2,2,96,3,128]{4,1,3,0,2:T(2,128)}), f32[2,2,96,3,128]{4,1,3,0,2:T(2,128)}, u32[]{:S(2)}, u32[]{:S(2)}) async-start(f32[2,2,96,3,128]{4,1,3,0,2:T(2,128)} %copy.155), calls=%async_computation.1 | async-start | bytes 1179648 | tf_op jit(solution)/shard_map/all_to_all | solution.py:105
  108.5 16.0 %all-to-all-start.3 = ((f32[2,2,96,3,128]{4,1,3,0,2:T(2,128)}), f32[2,2,96,3,128]{4,1,3,0,2:T(2,128)S(1)}, u32[]{:S(2)}, u32[]{:S(2)}) async-start(f32[2,2,96,3,128]{4,1,3,0,2:T(2,128)} %copy.169), calls=%async_computation.3 | async-start | bytes 1179648 | tf_op jit(solution)/shard_map/all_to_all | solution.py:105
  112.7 51.8 %all-gather.2.cloned.1.call-start = ((), (), s32[]{:S(2)}) async-start(), calls=%async_computation.10 | async-start | bytes 2826240 | tf_op jit(solution)/shard_map/all_gather | solution.py:259
  129.2 86.4 %reduce-scatter.5.cloned.1.call-start = ((), (), s32[]{:S(2)}) async-start(), calls=%async_computation.12 | async-start | bytes 2826240 | tf_op jit(solution)/shard_map/reduce_scatter | solution.py:153
  183.1 65.8 %reduce-scatter.3.cloned.1.call-start = ((), (), s32[]{:S(2)}) async-start(), calls=%async_computation.11 | async-start | bytes 2826240 | tf_op jit(solution)/shard_map/reduce_scatter | solution.py:153
  190.9 58.1 %copy-start.4 = (bf16[2,3,180,256]{3,2,1,0:T(8,128)(2,1)S(1)}, bf16[2,3,180,256]{3,2,1,0:T(8,128)(2,1)}, u32[]{:S(2)}) copy-start(bf16[2,3,180,256]{3,2,1,0:T(8,128)(2,1)} %fusion.102) | copy-start | bytes 1658884
  190.9 58.1 %copy-start.34 = (bf16[2,3,180,256]{3,0,2,1:T(2,128)(2,1)S(1)}, bf16[2,3,180,256]{3,0,2,1:T(2,128)(2,1)}, u32[]{:S(2)}) copy-start(bf16[2,3,180,256]{3,0,2,1:T(2,128)(2,1)} %param.9) | copy-start | bytes 1658884
  190.9 60.6 %copy-start.30 = (f32[180,91]{1,0:T(8,128)S(1)}, f32[180,91]{1,0:T(8,128)}, u32[]{:S(2)}) copy-start(f32[180,91]{1,0:T(8,128)} %copy-done.29) | copy-start | bytes 196564
  190.9 3.8 %collective-permute-start.5 = (f32[2,2,3,180]{3,2,1,0:T(4,128)S(1)}, f32[2,2,3,180]{3,2,1,0:T(4,128)S(1)}, u32[]{:S(2)}, u32[]{:S(2)}) collective-permute-start(f32[2,2,3,180]{3,2,1,0:T(4,128)S(1)} %pad_maximum_fusion.9), channel_id=1, source_target_pairs={{0,1},{1,0},{2,3},{3,2},{4,5},{5,4},{6,7},{7,6},{8,9},{9,8},{10,11... | collective-permute-start | bytes 25928 | tf_op jit(solution)/shard_map/ppermute | solution.py:127
  194.7 5.6 %collective-permute-start.6 = (f32[2,2,3,180]{3,2,1,0:T(4,128)S(1)}, f32[2,2,3,180]{3,2,1,0:T(4,128)S(1)}, u32[]{:S(2)}, u32[]{:S(2)}) collective-permute-start(f32[2,2,3,180]{3,2,1,0:T(4,128)S(1)} %fusion.550), channel_id=1, source_target_pairs={{0,2},{1,3},{2,0},{3,1},{4,6},{5,7},{6,4},{7,5},{8,10},{9,11},{10,... | collective-permute-start | bytes 25928 | tf_op jit(solution)/shard_map/ppermute | solution.py:127
  253.7 19.5 %all-to-all-start.6 = ((f32[2,2,3,96,128]{4,1,2,0,3:T(2,128)}), f32[2,2,3,96,128]{4,1,2,0,3:T(2,128)S(1)}, u32[]{:S(2)}, u32[]{:S(2)}) async-start(f32[2,2,3,96,128]{4,1,2,0,3:T(2,128)} %copy.194), calls=%async_computation.8 | async-start | bytes 1179648 | tf_op jit(solution)/shard_map/all_to_all | solution.py:99
  273.2 15.9 %all-to-all-start.4 = ((f32[2,2,3,96,128]{4,1,2,0,3:T(2,128)}), f32[2,2,3,96,128]{4,1,2,0,3:T(2,128)S(1)}, u32[]{:S(2)}, u32[]{:S(2)}) async-start(f32[2,2,3,96,128]{4,1,2,0,3:T(2,128)} %copy.180), calls=%async_computation.6 | async-start | bytes 1179648 | tf_op jit(solution)/shard_map/all_to_all | solution.py:99
  299.7 16.7 %all-to-all-start.5 = ((f32[2,2,96,3,128]{4,1,3,0,2:T(2,128)}), f32[2,2,96,3,128]{4,1,3,0,2:T(2,128)}, u32[]{:S(2)}, u32[]{:S(2)}) async-start(f32[2,2,96,3,128]{4,1,3,0,2:T(2,128)} %copy.188), calls=%async_computation.7 | async-start | bytes 1179648 | tf_op jit(solution)/shard_map/all_to_all | solution.py:105
  316.4 18.8 %all-to-all-start.7 = ((f32[2,2,96,3,128]{4,1,3,0,2:T(2,128)}), f32[2,2,96,3,128]{4,1,3,0,2:T(2,128)S(1)}, u32[]{:S(2)}, u32[]{:S(2)}) async-start(f32[2,2,96,3,128]{4,1,3,0,2:T(2,128)} %copy.202), calls=%async_computation.9 | async-start | bytes 1179648 | tf_op jit(solution)/shard_map/all_to_all | solution.py:105
  338.5 3.8 %collective-permute-start.7 = (f32[2,2,3,180]{3,2,1,0:T(4,128)S(1)}, f32[2,2,3,180]{3,2,1,0:T(4,128)S(1)}, u32[]{:S(2)}, u32[]{:S(2)}) collective-permute-start(f32[2,2,3,180]{3,2,1,0:T(4,128)S(1)} %pad_maximum_fusion.10), channel_id=1, source_target_pairs={{0,1},{1,0},{2,3},{3,2},{4,5},{5,4},{6,7},{7,6},{8,9},{9,8},{10,11... | collective-permute-start | bytes 25928 | tf_op jit(solution)/shard_map/ppermute | solution.py:127
  342.3 5.3 %collective-permute-start.8 = (f32[2,2,3,180]{3,2,1,0:T(4,128)S(1)}, f32[2,2,3,180]{3,2,1,0:T(4,128)S(1)}, u32[]{:S(2)}, u32[]{:S(2)}) collective-permute-start(f32[2,2,3,180]{3,2,1,0:T(4,128)S(1)} %fusion.549), channel_id=1, source_target_pairs={{0,2},{1,3},{2,0},{3,1},{4,6},{5,7},{6,4},{7,5},{8,10},{9,11},{10,... | collective-permute-start | bytes 25928 | tf_op jit(solution)/shard_map/ppermute | solution.py:127
  (42 other events, 226.8 us)
Sparse Core Ops, SparseCore 0:
  129.3 35.1 all-gather.1
  183.2 32.3 reduce-scatter.4
  218.2 30.7 reduce-scatter.2
where the time goes:
time: 363 us; the launch traced here: 356 us
  waiting for transfers between devices  163 us (45%)
  matrix products  68.6 us (19%)
  starting transfers between devices  61 us (17%)
  local copies, waits for them, and re-layouts  35.2 us (10%)
  between operations  15.7 us (4%)
  other arithmetic  12.5 us (3%)
    reduce_scatter x2, waiting for transfers between devices, channel_share(): lax.psum_scatter(term.astype(jnp.bfloat16), 'feat', scatter_dimension=3,...  48.5 us
    all_to_all x4, waiting for transfers between devices, to_columns(): moved = lax.all_to_all(stacked, 'space', 3, 2, tiled=True)  32 us
    ppermute x6, waiting for transfers between devices, token_sums(): lax.ppermute(pair, 'feat', [(i, i ^ bit) for i in range(count)])  31.4 us
    all_gather x1, waiting for transfers between devices, per_device(): whole_residual = lax.all_gather(residual, 'feat', axis=3, tiled=True)  26.5 us
    all_to_all x4, waiting for transfers between devices, to_rows(): moved = lax.all_to_all(stacked, 'space', 2, 3, tiled=True)  24.9 us
    all_to_all x4, starting transfers between devices, to_columns(): moved = lax.all_to_all(stacked, 'space', 3, 2, tiled=True)  24.7 us
    dot_general x32, matrix products, lat_apply(): return jnp.einsum('gh,bhkc->bgkc', table, field, precision=HIGHEST)  20.6 us
    all_to_all x4, starting transfers between devices, to_rows(): moved = lax.all_to_all(stacked, 'space', 2, 3, tiled=True)  20.6 us
  transfers between devices with their start and end apart: 20, of which 17 were waited for; matrix products, arithmetic and copies ran while one was open for 20% of the time, Pallas kernels for 0%

commit v1 on v0

--- a/solution.py
+++ b/solution.py
@@ -256,7 +256,9 @@
     )
     residual = (filtered + normed + values).astype(jnp.bfloat16)
     residual_vals = residual.astype(jnp.float32)
-    whole_residual = lax.all_gather(residual, "feat", axis=3, tiled=True)
+    whole_residual = jnp.concatenate(
+        lax.all_to_all(jnp.stack(lax.axis_size("feat") * [residual], axis=0), "feat", 0, 0), axis=3
+    )
     whole_vals = whole_residual.astype(jnp.float32)
     mean_two = jnp.sum(whole_vals, axis=-1, keepdims=True) / full_width
     square_two = jnp.sum(whole_vals * whole_vals, axis=-1, keepdims=True) / full_width

time: 363 us -> 379 us (1.044)
  local copies, waits for them, and re-layouts: 35.2 us -> 51 us
  waiting for transfers between devices: 163 us -> 153 us
  other arithmetic: 12.5 us -> 17.7 us
    all_gather x1 -> x0, waiting for transfers between devices: 26.5 us -> none  [per_device(): whole_residual = lax.all_gather(residual, 'feat', axis=3, tiled=True)]
    all_to_all x0 -> x1, waiting for transfers between devices: none -> 19.9 us  [per_device(): lax.all_to_all(jnp.stack(lax.axis_size('feat') * [residual], axis=0), 'fe...]
    convert_element_type x0 -> x3, local copies, waits for them, and re-layouts: none -> 11.1 us  [the longest x2 10.7 us: per_device(): whole_vals = whole_residual.astype(jnp.float32)]
    reduce_scatter x2, waiting for transfers between devices: 48.5 us -> 43 us  [channel_share(): lax.psum_scatter(term.astype(jnp.bfloat16), 'feat', scatter_dimension=3,...]
    all_to_all x0 -> x1, starting transfers between devices: none -> 5.32 us  [per_device(): lax.all_to_all(jnp.stack(lax.axis_size('feat') * [residual], axis=0), 'fe...]
  transfers between devices with their start and end apart: 20 -> 20, of which waited for: 17 -> 17; matrix products, arithmetic and copies ran while one was open for 20% -> 19% of each run, Pallas kernels for 0% -> 0%
where the time goes in v1:
time: 379 us; the launch traced here: 372 us
  waiting for transfers between devices  153 us (40%)
  matrix products  71.1 us (19%)
  starting transfers between devices  64 us (17%)
  local copies, waits for them, and re-layouts  51 us (13%)
  other arithmetic  17.7 us (5%)
  between operations  16.1 us (4%)
    reduce_scatter x2, waiting for transfers between devices, channel_share(): lax.psum_scatter(term.astype(jnp.bfloat16), 'feat', scatter_dimension=3,...  43 us
    ppermute x6, waiting for transfers between devices, token_sums(): lax.ppermute(pair, 'feat', [(i, i ^ bit) for i in range(count)])  33.6 us
    all_to_all x4, waiting for transfers between devices, to_columns(): moved = lax.all_to_all(stacked, 'space', 3, 2, tiled=True)  31.3 us
    all_to_all x4, waiting for transfers between devices, to_rows(): moved = lax.all_to_all(stacked, 'space', 2, 3, tiled=True)  24.9 us
    all_to_all x4, starting transfers between devices, to_columns(): moved = lax.all_to_all(stacked, 'space', 3, 2, tiled=True)  24.5 us
    all_to_all x4, starting transfers between devices, to_rows(): moved = lax.all_to_all(stacked, 'space', 2, 3, tiled=True)  20.7 us
    dot_general x32, matrix products, lat_apply(): return jnp.einsum('gh,bhkc->bgkc', table, field, precision=HIGHEST)  20.6 us
    all_to_all x1, waiting for transfers between devices, per_device(): lax.all_to_all(jnp.stack(lax.axis_size('feat') * [residual], axis=0), 'fe...  19.9 us
  transfers between devices with their start and end apart: 20, of which 17 were waited for; matrix products, arithmetic and copies ran while one was open for 19% of the time, Pallas kernels for 0%

profile of v1, /device:TPU:0, one launch (start us, length us, event | category | flops | bytes accessed | tf_op | source)
XLA Modules:
  0.0 372.4 jit_solution(5834565305347689990)
XLA Ops:
  17.2 17.7 %collective-permute-done = f32[2,2,3,180]{3,1,2,0:T(2,128)S(1)} collective-permute-done((f32[2,2,3,180]{3,1,2,0:T(2,128)S(1)}, f32[2,2,3,180]{3,1,2,0:T(2,128)S(1)}, u32[]{:S(2)}, u32[]{:S(2)}) %collective-permute-start) | collective-permute-done | bytes 8672 | tf_op jit(solution)/shard_map/ppermute | solution.py:127
  43.9 8.3 %all-to-all-start = ((f32[2,2,3,96,128]{4,1,2,0,3:T(2,128)}), f32[2,2,3,96,128]{4,1,2,0,3:T(2,128)}, u32[]{:S(2)}, u32[]{:S(2)}) async-start(f32[2,2,3,96,128]{4,1,2,0,3:T(2,128)} %copy.388), calls=%async_computation | async-start | bytes 1179648 | tf_op jit(solution)/shard_map/all_to_all | solution.py:99
  55.1 8.9 %all-to-all-done = f32[2,2,3,96,128]{4,1,2,0,3:T(2,128)} async-done(((f32[2,2,3,96,128]{4,1,2,0,3:T(2,128)}), f32[2,2,3,96,128]{4,1,2,0,3:T(2,128)}, u32[]{:S(2)}, u32[]{:S(2)}) %all-to-all-start) | async-done | bytes 589856 | tf_op jit(solution)/shard_map/all_to_all | solution.py:99
  64.0 4.7 %all-to-all-start.2 = ((f32[2,2,3,96,128]{4,1,2,0,3:T(2,128)}), f32[2,2,3,96,128]{4,1,2,0,3:T(2,128)S(1)}, u32[]{:S(2)}, u32[]{:S(2)}) async-start(f32[2,2,3,96,128]{4,1,2,0,3:T(2,128)} %copy.402), calls=%async_computation.2 | async-start | bytes 1179648 | tf_op jit(solution)/shard_map/all_to_all | solution.py:99
  92.0 4.6 %all-to-all-start.1 = ((f32[2,2,96,3,128]{4,1,3,0,2:T(2,128)}), f32[2,2,96,3,128]{4,1,3,0,2:T(2,128)}, u32[]{:S(2)}, u32[]{:S(2)}) async-start(f32[2,2,96,3,128]{4,1,3,0,2:T(2,128)} %copy.396), calls=%async_computation.1 | async-start | bytes 1179648 | tf_op jit(solution)/shard_map/all_to_all | solution.py:105
  102.9 5.6 %all-to-all-done.1 = f32[2,2,96,3,128]{4,1,3,0,2:T(2,128)} async-done(((f32[2,2,96,3,128]{4,1,3,0,2:T(2,128)}), f32[2,2,96,3,128]{4,1,3,0,2:T(2,128)}, u32[]{:S(2)}, u32[]{:S(2)}) %all-to-all-start.1) | async-done | bytes 589856 | tf_op jit(solution)/shard_map/all_to_all | solution.py:105
  108.4 4.1 %all-to-all-start.3 = ((f32[2,2,96,3,128]{4,1,3,0,2:T(2,128)}), f32[2,2,96,3,128]{4,1,3,0,2:T(2,128)S(1)}, u32[]{:S(2)}, u32[]{:S(2)}) async-start(f32[2,2,96,3,128]{4,1,3,0,2:T(2,128)} %copy.410), calls=%async_computation.3 | async-start | bytes 1179648 | tf_op jit(solution)/shard_map/all_to_all | solution.py:105
  115.5 8.9 %all-to-all-done.3 = f32[2,2,96,3,128]{4,1,3,0,2:T(2,128)S(1)} async-done(((f32[2,2,96,3,128]{4,1,3,0,2:T(2,128)}), f32[2,2,96,3,128]{4,1,3,0,2:T(2,128)S(1)}, u32[]{:S(2)}, u32[]{:S(2)}) %all-to-all-start.3) | async-done | bytes 589856 | tf_op jit(solution)/shard_map/all_to_all | solution.py:105
  132.0 5.3 %all-to-all-start.4 = ((bf16[4,2,3,180,256]{4,1,3,2,0:T(2,128)(2,1)}), bf16[4,2,3,180,256]{4,1,3,2,0:T(2,128)(2,1)}, u32[]{:S(2)}, u32[]{:S(2)}) async-start(bf16[4,2,3,180,256]{4,1,3,2,0:T(2,128)(2,1)} %stack.121), calls=%async_computation.4 | async-start | bytes 4423680 | tf_op jit(solution)/shard_map/all_to_all | solution.py:260
  146.3 19.9 %all-to-all-done.4 = bf16[4,2,3,180,256]{4,1,3,2,0:T(2,128)(2,1)} async-done(((bf16[4,2,3,180,256]{4,1,3,2,0:T(2,128)(2,1)}), bf16[4,2,3,180,256]{4,1,3,2,0:T(2,128)(2,1)}, u32[]{:S(2)}, u32[]{:S(2)}) %all-to-all-start.4) | async-done | bytes 2211872 | tf_op jit(solution)/shard_map/all_to_all | solution.py:260
  166.1 5.4 %fusion.18 = (f32[2,3,180]{0,2,1:T(8,128)S(1)}, f32[2,3,180]{0,2,1:T(8,128)S(1)}) fusion(bf16[4,2,3,180,256]{4,1,3,2,0:T(2,128)(2,1)} %all-to-all-done.4), kind=kLoop, calls=%fused_computation.23 | loop fusion | flops 4421520 | bytes 2220480 | tf_op jit(solution)/shard_map/reduce_sum | solution.py:263
  178.8 6.9 %reshape.436 = f32[2,3,180,1024]{3,2,1,0:T(8,128)} reshape(f32[2,3,180,4,256]{4,3,2,1,0:T(4,128)} %copy.417) | data formatting | bytes 8847360 | tf_op jit(solution)/shard_map/convert_element_type | solution.py:262
  185.7 7.1 %fusion.7 = f32[2,3,180,1024]{3,2,1,0:T(8,128)} fusion(f32[2,3,180,1024]{3,2,1,0:T(8,128)} %reshape.436, f32[2,3,180]{2,1,0:T(4,128)S(1)} %get-tuple-element.60, f32[2,3,180]{2,1,0:T(4,128)S(1)} %get-tuple-element.59, bf16[1024,1024]{1,0:T(8,128)(2,1)S(1)} %copy-done), kind=kOutput, calls=%fused_computation.14 | convolution fusion | flops 2268241920 | bytes 10953152 | tf_op jit(solution)/shard_map/brwd,dh->brwh/dot_general | solution.py:267
  192.9 11.3 %fusion.546 = (f32[2,3,180]{2,1,0:T(4,128)S(1)}, f32[2,3,180]{2,1,0:T(4,128)S(1)}, bf16[2,3,180,1024]{3,2,1,0:T(8,128)(2,1)}) fusion(f32[2,3,180]{2,1,0:T(4,128)S(1)} %get-tuple-element.60, f32[2,3,180,1024]{3,2,1,0:T(8,128)} %reshape.436, f32[2,3,180]{2,1,0:T(4,128)S(1)} %get-tuple-element.59, bf16[1024,1024]{1,0:T(8,128)(2,1)S(1)} %copy-done, ...), kind=kOutput, calls=%fused_computation.645 | convolution fusion | flops 4547540992 | bytes 17482624 | tf_op jit(solution)/shard_map/brwh,dh->brwd/dot_general | solution.py:279
  205.8 6.2 %fusion.24 = bf16[2,3,180,1024]{3,2,1,0:T(8,128)(2,1)} fusion(bf16[1024,1024]{1,0:T(8,128)(2,1)S(1)} %copy-done.46, f32[2,3,180,1024]{3,2,1,0:T(8,128)} %fusion.7), kind=kOutput, calls=%fused_computation.33 | convolution fusion | flops 2271559680 | bytes 8732672 | tf_op jit(solution)/shard_map/brwh,hd->brwd/dot_general | solution.py:271
  216.7 5.1 %collective-permute-done.6 = f32[2,2,3,180]{3,1,2,0:T(2,128)S(1)} collective-permute-done((f32[2,2,3,180]{3,1,2,0:T(2,128)S(1)}, f32[2,2,3,180]{3,1,2,0:T(2,128)S(1)}, u32[]{:S(2)}, u32[]{:S(2)}) %collective-permute-start.6) | collective-permute-done | bytes 8672 | tf_op jit(solution)/shard_map/ppermute | solution.py:127
  221.8 9.6 %reduce-scatter.5.cloned.1.call-done = bf16[2,3,180,256]{3,2,1,0:T(8,128)(2,1)} async-done(((bf16[2,3,180,1024]{3,2,1,0:T(8,128)(2,1)}), bf16[2,3,180,256]{3,2,1,0:T(8,128)(2,1)}) %reduce-scatter.5.cloned.1.call-update) | async-done | bytes 552976 | tf_op jit(solution)/shard_map/reduce_scatter | solution.py:153
  231.4 33.4 %reduce-scatter.3.cloned.1.call-done = bf16[2,3,180,256]{3,2,1,0:T(8,128)(2,1)} async-done(((bf16[2,3,180,1024]{3,2,1,0:T(8,128)(2,1)}), bf16[2,3,180,256]{3,2,1,0:T(8,128)(2,1)}) %reduce-scatter.3.cloned.1.call-update) | async-done | bytes 552976 | tf_op jit(solution)/shard_map/reduce_scatter | solution.py:153
  269.6 7.4 %all-to-all-start.7 = ((f32[2,2,3,96,128]{4,1,2,0,3:T(2,128)}), f32[2,2,3,96,128]{4,1,2,0,3:T(2,128)S(1)}, u32[]{:S(2)}, u32[]{:S(2)}) async-start(f32[2,2,3,96,128]{4,1,2,0,3:T(2,128)} %copy.443), calls=%async_computation.9 | async-start | bytes 1179648 | tf_op jit(solution)/shard_map/all_to_all | solution.py:99
  279.2 9.6 %all-to-all-done.7 = f32[2,2,3,96,128]{4,1,2,0,3:T(2,128)S(1)} async-done(((f32[2,2,3,96,128]{4,1,2,0,3:T(2,128)}), f32[2,2,3,96,128]{4,1,2,0,3:T(2,128)S(1)}, u32[]{:S(2)}, u32[]{:S(2)}) %all-to-all-start.7) | async-done | bytes 589856 | tf_op jit(solution)/shard_map/all_to_all | solution.py:99
  294.8 9.9 %all-to-all-done.5 = f32[2,2,3,96,128]{4,1,2,0,3:T(2,128)S(1)} async-done(((f32[2,2,3,96,128]{4,1,2,0,3:T(2,128)}), f32[2,2,3,96,128]{4,1,2,0,3:T(2,128)S(1)}, u32[]{:S(2)}, u32[]{:S(2)}) %all-to-all-start.5) | async-done | bytes 589856 | tf_op jit(solution)/shard_map/all_to_all | solution.py:99
  315.2 5.0 %all-to-all-start.6 = ((f32[2,2,96,3,128]{4,1,3,0,2:T(2,128)}), f32[2,2,96,3,128]{4,1,3,0,2:T(2,128)}, u32[]{:S(2)}, u32[]{:S(2)}) async-start(f32[2,2,96,3,128]{4,1,3,0,2:T(2,128)} %copy.437), calls=%async_computation.8 | async-start | bytes 1179648 | tf_op jit(solution)/shard_map/all_to_all | solution.py:105
  332.0 7.0 %all-to-all-start.8 = ((f32[2,2,96,3,128]{4,1,3,0,2:T(2,128)}), f32[2,2,96,3,128]{4,1,3,0,2:T(2,128)S(1)}, u32[]{:S(2)}, u32[]{:S(2)}) async-start(f32[2,2,96,3,128]{4,1,3,0,2:T(2,128)} %copy.451), calls=%async_computation.10 | async-start | bytes 1179648 | tf_op jit(solution)/shard_map/all_to_all | solution.py:105
  341.3 9.5 %all-to-all-done.8 = f32[2,2,96,3,128]{4,1,3,0,2:T(2,128)S(1)} async-done(((f32[2,2,96,3,128]{4,1,3,0,2:T(2,128)}), f32[2,2,96,3,128]{4,1,3,0,2:T(2,128)S(1)}, u32[]{:S(2)}, u32[]{:S(2)}) %all-to-all-start.8) | async-done | bytes 589856 | tf_op jit(solution)/shard_map/all_to_all | solution.py:105
  (290 shorter events, 135.1 us)
Async XLA Ops:
  7.2 178.5 %copy-start = (bf16[1024,1024]{1,0:T(8,128)(2,1)S(1)}, bf16[1024,1024]{1,0:T(8,128)(2,1)}, u32[]{:S(2)}) copy-start(bf16[1024,1024]{1,0:T(8,128)(2,1)} %param.14) | copy-start | bytes 6291460
  7.2 94.3 %collective-permute-start.4 = (bf16[2,3,180,256]{3,0,2,1:T(2,128)(2,1)}, bf16[2,3,180,256]{3,0,2,1:T(2,128)(2,1)}, u32[]{:S(2)}, u32[]{:S(2)}) collective-permute-start(bf16[2,3,180,256]{3,0,2,1:T(2,128)(2,1)} %param.9), channel_id=1, source_target_pairs={{0,3},{1,0},{2,1},{3,2},{4,7},{5,4},{6,5},{7,6},{8,11},{9,8},{10,9... | collective-permute-start | bytes 1658888 | tf_op jit(solution)/shard_map/ppermute | solution.py:135
  10.3 91.2 %collective-permute-start.3 = (bf16[2,3,180,256]{3,0,2,1:T(2,128)(2,1)}, bf16[2,3,180,256]{3,0,2,1:T(2,128)(2,1)}, u32[]{:S(2)}, u32[]{:S(2)}) collective-permute-start(bf16[2,3,180,256]{3,0,2,1:T(2,128)(2,1)} %param.9), channel_id=1, source_target_pairs={{0,2},{1,3},{2,0},{3,1},{4,6},{5,7},{6,4},{7,5},{8,10},{9,11},{10,... | collective-permute-start | bytes 1658888 | tf_op jit(solution)/shard_map/ppermute | solution.py:135
  11.0 90.6 %collective-permute-start.2 = (bf16[2,3,180,256]{3,0,2,1:T(2,128)(2,1)}, bf16[2,3,180,256]{3,0,2,1:T(2,128)(2,1)}, u32[]{:S(2)}, u32[]{:S(2)}) collective-permute-start(bf16[2,3,180,256]{3,0,2,1:T(2,128)(2,1)} %param.9), channel_id=1, source_target_pairs={{0,1},{1,2},{2,3},{3,0},{4,5},{5,6},{6,7},{7,4},{8,9},{9,10},{10,1... | collective-permute-start | bytes 1658888 | tf_op jit(solution)/shard_map/ppermute | solution.py:135
  13.5 21.3 %collective-permute-start = (f32[2,2,3,180]{3,1,2,0:T(2,128)S(1)}, f32[2,2,3,180]{3,1,2,0:T(2,128)S(1)}, u32[]{:S(2)}, u32[]{:S(2)}) collective-permute-start(f32[2,2,3,180]{3,1,2,0:T(2,128)S(1)} %copy.384), channel_id=1, source_target_pairs={{0,1},{1,0},{2,3},{3,2},{4,5},{5,4},{6,7},{7,6},{8,9},{9,8},{10,11... | collective-permute-start | bytes 25928 | tf_op jit(solution)/shard_map/ppermute | solution.py:127
  34.9 5.3 %collective-permute-start.1 = (f32[2,2,3,180]{3,1,2,0:T(2,128)S(1)}, f32[2,2,3,180]{3,1,2,0:T(2,128)S(1)}, u32[]{:S(2)}, u32[]{:S(2)}) collective-permute-start(f32[2,2,3,180]{3,1,2,0:T(2,128)S(1)} %copy.386), channel_id=1, source_target_pairs={{0,2},{1,3},{2,0},{3,1},{4,6},{5,7},{6,4},{7,5},{8,10},{9,11},{10,... | collective-permute-start | bytes 25928 | tf_op jit(solution)/shard_map/ppermute | solution.py:127
  43.9 20.1 %all-to-all-start = ((f32[2,2,3,96,128]{4,1,2,0,3:T(2,128)}), f32[2,2,3,96,128]{4,1,2,0,3:T(2,128)}, u32[]{:S(2)}, u32[]{:S(2)}) async-start(f32[2,2,3,96,128]{4,1,2,0,3:T(2,128)} %copy.388), calls=%async_computation | async-start | bytes 1179648 | tf_op jit(solution)/shard_map/all_to_all | solution.py:99
  64.0 16.0 %all-to-all-start.2 = ((f32[2,2,3,96,128]{4,1,2,0,3:T(2,128)}), f32[2,2,3,96,128]{4,1,2,0,3:T(2,128)S(1)}, u32[]{:S(2)}, u32[]{:S(2)}) async-start(f32[2,2,3,96,128]{4,1,2,0,3:T(2,128)} %copy.402), calls=%async_computation.2 | async-start | bytes 1179648 | tf_op jit(solution)/shard_map/all_to_all | solution.py:99
  92.0 16.4 %all-to-all-start.1 = ((f32[2,2,96,3,128]{4,1,3,0,2:T(2,128)}), f32[2,2,96,3,128]{4,1,3,0,2:T(2,128)}, u32[]{:S(2)}, u32[]{:S(2)}) async-start(f32[2,2,96,3,128]{4,1,3,0,2:T(2,128)} %copy.396), calls=%async_computation.1 | async-start | bytes 1179648 | tf_op jit(solution)/shard_map/all_to_all | solution.py:105
  108.4 16.0 %all-to-all-start.3 = ((f32[2,2,96,3,128]{4,1,3,0,2:T(2,128)}), f32[2,2,96,3,128]{4,1,3,0,2:T(2,128)S(1)}, u32[]{:S(2)}, u32[]{:S(2)}) async-start(f32[2,2,96,3,128]{4,1,3,0,2:T(2,128)} %copy.410), calls=%async_computation.3 | async-start | bytes 1179648 | tf_op jit(solution)/shard_map/all_to_all | solution.py:105
  132.0 34.1 %all-to-all-start.4 = ((bf16[4,2,3,180,256]{4,1,3,2,0:T(2,128)(2,1)}), bf16[4,2,3,180,256]{4,1,3,2,0:T(2,128)(2,1)}, u32[]{:S(2)}, u32[]{:S(2)}) async-start(bf16[4,2,3,180,256]{4,1,3,2,0:T(2,128)(2,1)} %stack.121), calls=%async_computation.4 | async-start | bytes 4423680 | tf_op jit(solution)/shard_map/all_to_all | solution.py:260
  137.4 94.1 %reduce-scatter.5.cloned.1.call-start = ((), (), s32[]{:S(2)}) async-start(), calls=%async_computation.12 | async-start | bytes 2826240 | tf_op jit(solution)/shard_map/reduce_scatter | solution.py:153
  204.2 60.5 %reduce-scatter.3.cloned.1.call-start = ((), (), s32[]{:S(2)}) async-start(), calls=%async_computation.11 | async-start | bytes 2826240 | tf_op jit(solution)/shard_map/reduce_scatter | solution.py:153
  212.0 52.8 %copy-start.5 = (bf16[2,3,180,256]{3,2,1,0:T(8,128)(2,1)S(1)}, bf16[2,3,180,256]{3,2,1,0:T(8,128)(2,1)}, u32[]{:S(2)}) copy-start(bf16[2,3,180,256]{3,2,1,0:T(8,128)(2,1)} %copy-done.4) | copy-start | bytes 1658884
  212.0 52.8 %copy-start.35 = (bf16[2,3,180,256]{3,0,2,1:T(2,128)(2,1)S(1)}, bf16[2,3,180,256]{3,0,2,1:T(2,128)(2,1)}, u32[]{:S(2)}) copy-start(bf16[2,3,180,256]{3,0,2,1:T(2,128)(2,1)} %param.9) | copy-start | bytes 1658884
  212.0 55.3 %copy-start.32 = (f32[180,91]{1,0:T(8,128)S(1)}, f32[180,91]{1,0:T(8,128)}, u32[]{:S(2)}) copy-start(f32[180,91]{1,0:T(8,128)} %copy-done.31) | copy-start | bytes 196564
  212.0 4.0 %collective-permute-start.5 = (f32[2,2,3,180]{3,1,2,0:T(2,128)S(1)}, f32[2,2,3,180]{3,1,2,0:T(2,128)S(1)}, u32[]{:S(2)}, u32[]{:S(2)}) collective-permute-start(f32[2,2,3,180]{3,1,2,0:T(2,128)S(1)} %copy.425), channel_id=1, source_target_pairs={{0,1},{1,0},{2,3},{3,2},{4,5},{5,4},{6,7},{7,6},{8,9},{9,8},{10,11... | collective-permute-start | bytes 25928 | tf_op jit(solution)/shard_map/ppermute | solution.py:127
  216.1 5.7 %collective-permute-start.6 = (f32[2,2,3,180]{3,1,2,0:T(2,128)S(1)}, f32[2,2,3,180]{3,1,2,0:T(2,128)S(1)}, u32[]{:S(2)}, u32[]{:S(2)}) collective-permute-start(f32[2,2,3,180]{3,1,2,0:T(2,128)S(1)} %copy.427), channel_id=1, source_target_pairs={{0,2},{1,3},{2,0},{3,1},{4,6},{5,7},{6,4},{7,5},{8,10},{9,11},{10,... | collective-permute-start | bytes 25928 | tf_op jit(solution)/shard_map/ppermute | solution.py:127
  269.6 19.2 %all-to-all-start.7 = ((f32[2,2,3,96,128]{4,1,2,0,3:T(2,128)}), f32[2,2,3,96,128]{4,1,2,0,3:T(2,128)S(1)}, u32[]{:S(2)}, u32[]{:S(2)}) async-start(f32[2,2,3,96,128]{4,1,2,0,3:T(2,128)} %copy.443), calls=%async_computation.9 | async-start | bytes 1179648 | tf_op jit(solution)/shard_map/all_to_all | solution.py:99
  288.8 15.9 %all-to-all-start.5 = ((f32[2,2,3,96,128]{4,1,2,0,3:T(2,128)}), f32[2,2,3,96,128]{4,1,2,0,3:T(2,128)S(1)}, u32[]{:S(2)}, u32[]{:S(2)}) async-start(f32[2,2,3,96,128]{4,1,2,0,3:T(2,128)} %copy.429), calls=%async_computation.7 | async-start | bytes 1179648 | tf_op jit(solution)/shard_map/all_to_all | solution.py:99
  315.2 16.8 %all-to-all-start.6 = ((f32[2,2,96,3,128]{4,1,3,0,2:T(2,128)}), f32[2,2,96,3,128]{4,1,3,0,2:T(2,128)}, u32[]{:S(2)}, u32[]{:S(2)}) async-start(f32[2,2,96,3,128]{4,1,3,0,2:T(2,128)} %copy.437), calls=%async_computation.8 | async-start | bytes 1179648 | tf_op jit(solution)/shard_map/all_to_all | solution.py:105
  332.0 18.8 %all-to-all-start.8 = ((f32[2,2,96,3,128]{4,1,3,0,2:T(2,128)}), f32[2,2,96,3,128]{4,1,3,0,2:T(2,128)S(1)}, u32[]{:S(2)}, u32[]{:S(2)}) async-start(f32[2,2,96,3,128]{4,1,3,0,2:T(2,128)} %copy.451), calls=%async_computation.10 | async-start | bytes 1179648 | tf_op jit(solution)/shard_map/all_to_all | solution.py:105
  354.1 3.8 %collective-permute-start.7 = (f32[2,2,3,180]{3,1,2,0:T(2,128)S(1)}, f32[2,2,3,180]{3,1,2,0:T(2,128)S(1)}, u32[]{:S(2)}, u32[]{:S(2)}) collective-permute-start(f32[2,2,3,180]{3,1,2,0:T(2,128)S(1)} %copy.457), channel_id=1, source_target_pairs={{0,1},{1,0},{2,3},{3,2},{4,5},{5,4},{6,7},{7,6},{8,9},{9,8},{10,11... | collective-permute-start | bytes 25928 | tf_op jit(solution)/shard_map/ppermute | solution.py:127
  357.9 5.3 %collective-permute-start.8 = (f32[2,2,3,180]{3,1,2,0:T(2,128)S(1)}, f32[2,2,3,180]{3,1,2,0:T(2,128)S(1)}, u32[]{:S(2)}, u32[]{:S(2)}) collective-permute-start(f32[2,2,3,180]{3,1,2,0:T(2,128)S(1)} %copy.459), channel_id=1, source_target_pairs={{0,2},{1,3},{2,0},{3,1},{4,6},{5,7},{6,4},{7,5},{8,10},{9,11},{10,... | collective-permute-start | bytes 25928 | tf_op jit(solution)/shard_map/ppermute | solution.py:127
  (43 other events, 228.1 us)
Sparse Core Ops, SparseCore 0:
  204.3 27.0 reduce-scatter.4
  234.0 30.7 reduce-scatter.2
